TPU v7x, 32 devices: a whole 2x2x4 slice. The times are simulated.
32 devices in a mesh: req: 8 (over y, x, core), head: 4 (over z).
Axes of the slice: x: 2, y: 2, z: 4, core: 2. Of those that a mesh axis runs over, the one named last changes fastest.
Arguments:
- queries: bfloat16 [4096, 8192], P('req', 'head'), may hold values from -150 to 150, as said below
- new_keys: bfloat16 [4096, 1024], P('req', 'head'), may hold values from -6 to 6, as said below
- fresh_values: bfloat16 [4096, 1024], P('req', 'head'), may hold values from -6 to 6
- key_page_pool: bfloat16 [224, 128, 1024], P('req', None, 'head'), may hold values from -6 to 6
- value_page_pool: bfloat16 [224, 128, 1024], P('req', None, 'head'), may hold values from -6 to 6
- page_table: int32 [16, 14], P('req'), may hold values from 0 to 27, as said below
- new_counts: int32 [16], P('req'), may hold values from 1 to 256, 2048 in all
- cached_lens: int32 [16], P('req'), may hold values from 1 to 1536, 8192 in all
- deal_offset: int32 [8], P('req'), may hold values from 0 to 7
- residual: bfloat16 [2112, 8192], P('req', 'head'), may hold values from -1.1953125 to 1.1953125
- out_weight: bfloat16 [8192, 8192], P('head', 'req'), may hold values from -0.09375 to 0.09375
Outputs:
- hidden: bfloat16 [2112, 8192], P('req', 'head')
- keys_out: bfloat16 [224, 128, 1024], P('req', None, 'head')
- values_out: bfloat16 [224, 128, 1024], P('req', None, 'head')
Inputs may be any that keep to these rules, and one draw needn't show every extreme that they name: `new_counts`: the counts sum to 2048; the largest is exactly 256. `cached_lens`: the counts sum to 8192; the largest is exactly 1536. `page_table`: the 2 rows of each aligned block of requests hold together each of 0 to 27 once. `queries`: real values. `new_keys`: real values.
All inputs are finite; a program needn't handle non-finite values. No bound on the sum of `new_counts` or of `cached_lens` on one device may be relied on, other than what follows from the above.
Results may differ from a plain program's by a relative error of at most 0.0085.
Values may be sent and summed in bfloat16 or wider, within the bound.
No kernel may reach another device: no remote copies, remote signals or barrier semaphores. Data moves between devices by JAX's collectives and lax.ppermute only.
A program may use at most 128 MiB of HBM per device.

v0:
```python
import math
import jax
import jax.numpy as jnp
from jax import lax
from jax.sharding import PartitionSpec as P

HEAD_SIZE = 128
NEGATIVE = -1e30


def head_attention(query_matrix, prior_keys, prior_values, visible, scale_factor):
    scores = (
        jnp.einsum("tkd,skd->kts", query_matrix, prior_keys, preferred_element_type=jnp.float32)
        * scale_factor
    )
    spots_all = jnp.arange(prior_keys.shape[0], dtype=jnp.int32)
    allowed = spots_all[None, None, :] <= visible[None, :, None]
    scores = jnp.where(allowed, scores, NEGATIVE)
    highest = jnp.max(scores, axis=2, keepdims=True)
    expo_terms = jnp.where(allowed, jnp.exp(scores - highest), 0.0)
    weights = (expo_terms / jnp.sum(expo_terms, axis=2, keepdims=True)).astype(jnp.bfloat16)
    mixed = jnp.einsum("kts,skd->tkd", weights, prior_values, preferred_element_type=jnp.float32)
    return mixed.astype(jnp.bfloat16)


def deal(row_block, new_counts, lead_in, shares, starts, totals, balanced):
    groups = lax.axis_size("req")
    my_rank = lax.axis_index("req")
    per_group = new_counts.shape[0]
    new_limit = row_block.shape[0] // per_group
    pair_slots = row_block.shape[0] // groups
    columns = row_block.shape[1]
    own_lead = lax.dynamic_index_in_dim(lead_in, my_rank, 0, keepdims=False)
    ordinal = jnp.arange(pair_slots, dtype=jnp.int32)[None, :] * groups + own_lead[:, None]
    ends_at = jnp.cumsum(new_counts)
    request_index = jnp.sum(
        (ordinal[:, :, None] >= ends_at[None, None, :]).astype(jnp.int32), axis=2
    )
    request_index = jnp.minimum(request_index, per_group - 1)
    before = ends_at - new_counts
    source = request_index * new_limit + ordinal - jnp.take(before, request_index)
    own_total = lax.dynamic_index_in_dim(totals, my_rank, 0, keepdims=False)
    is_live = ordinal < own_total
    source = jnp.where(is_live, source, 0)
    picked = jnp.take(row_block, source.reshape(-1), axis=0).reshape(groups, pair_slots, columns)
    outgoing = jnp.where(is_live[:, :, None], picked, jnp.zeros((), row_block.dtype))
    arrived = lax.all_to_all(outgoing, "req", split_axis=0, concat_axis=0, tiled=True)
    own_shares = lax.dynamic_index_in_dim(shares, my_rank, 1, keepdims=False)
    own_starts = lax.dynamic_index_in_dim(starts, my_rank, 1, keepdims=False)
    within = jnp.arange(pair_slots, dtype=jnp.int32)[None, :]
    landing = jnp.where(within < own_shares[:, None], own_starts[:, None] + within, balanced)
    blank_rows = jnp.zeros((balanced, columns), row_block.dtype)
    return blank_rows.at[landing.reshape(-1)].set(arrived.reshape(-1, columns), mode="drop")


def project(row_block, out_weight):
    return jnp.dot(
        row_block,
        lax.all_gather(out_weight, "req", axis=1, tiled=True),
        preferred_element_type=jnp.float32,
    )


def head_total(partial_sum):
    return lax.psum_scatter(
        partial_sum.astype(jnp.bfloat16), "head", scatter_dimension=1, tiled=True
    ).astype(jnp.float32)


def local(
    queries,
    new_keys,
    fresh_values,
    key_page_pool,
    value_page_pool,
    page_table,
    new_counts,
    cached_lens,
    deal_offset,
    residual,
    out_weight,
):
    groups = lax.axis_size("req")
    per_group = new_counts.shape[0]
    page_count = page_table.shape[1]
    page_rows = key_page_pool.shape[1]
    channel_count = key_page_pool.shape[2]
    kv_local = channel_count // HEAD_SIZE
    slot_count = queries.shape[0]
    new_limit = slot_count // per_group
    q_width = queries.shape[1]
    group_fanout = q_width // channel_count
    balanced = residual.shape[0]
    new_slot = jnp.arange(new_limit, dtype=jnp.int32)
    positions = cached_lens[:, None] + new_slot[None, :]
    page_of = jnp.take_along_axis(page_table, positions // page_rows, axis=1)
    outside = key_page_pool.shape[0] * page_rows
    target = jnp.where(
        new_slot[None, :] < new_counts[:, None],
        page_of * page_rows + positions % page_rows,
        outside,
    ).reshape(-1)
    flat_keys = key_page_pool.reshape(-1, channel_count).at[target].set(new_keys, mode="drop")
    flat_values = (
        value_page_pool.reshape(-1, channel_count).at[target].set(fresh_values, mode="drop")
    )
    gathered_keys = flat_keys.reshape(key_page_pool.shape)
    gathered_values = flat_values.reshape(value_page_pool.shape)
    scale_factor = 1.0 / math.sqrt(HEAD_SIZE)
    pieces = []
    for member in range(per_group):
        prior_keys = gathered_keys[page_table[member]].reshape(
            page_count * page_rows, kv_local, HEAD_SIZE
        )
        prior_values = gathered_values[page_table[member]].reshape(
            page_count * page_rows, kv_local, HEAD_SIZE
        )
        query_matrix = queries[member * new_limit : (member + 1) * new_limit].reshape(
            new_limit, kv_local, group_fanout, HEAD_SIZE
        )
        query_matrix = jnp.moveaxis(query_matrix, 2, 0)
        visible = positions[member]
        mixed = lax.map(
            lambda single: head_attention(single, prior_keys, prior_values, visible, scale_factor),
            query_matrix,
        )
        pieces.append(jnp.moveaxis(mixed, 0, 2).reshape(new_limit, q_width))
    attended = jnp.concatenate(pieces, axis=0)
    load_counts, offsets_all = (
        lax.all_gather(new_counts, "req", axis=0, tiled=True),
        lax.all_gather(deal_offset, "req", axis=0, tiled=True),
    )
    totals = jnp.sum(load_counts.reshape(groups, per_group), axis=1)
    rank_ids = jnp.arange(groups, dtype=jnp.int32)
    lead_in = jnp.remainder(rank_ids[None, :] - offsets_all[:, None], groups)
    shares = jnp.maximum((totals[:, None] - lead_in + groups - 1) // groups, 0)
    starts = jnp.cumsum(shares, axis=0) - shares
    summed = head_total(project(attended, out_weight)).astype(jnp.bfloat16)
    placed = deal(summed, new_counts, lead_in, shares, starts, totals, balanced)
    hidden = (residual.astype(jnp.float32) + placed.astype(jnp.float32)).astype(jnp.bfloat16)
    return (hidden, gathered_keys, gathered_values)


def solution(mesh):
    placed = (
        P("req", "head"),
        P("req", "head"),
        P("req", "head"),
        P("req", None, "head"),
        P("req", None, "head"),
        P("req", None),
        P("req"),
        P("req"),
        P("req"),
        P("req", "head"),
        P("head", "req"),
    )
    return jax.shard_map(
        local,
        mesh=mesh,
        in_specs=placed,
        out_specs=(P("req", "head"), P("req", None, "head"), P("req", None, "head")),
        check_vma=False,
    )
```

profile of v0, /device:TPU:0, one launch (start us, length us, event | category | flops | bytes accessed | tf_op | source)
XLA Modules:
  0.0 404.9 jit_solution(16835856660951470666)
XLA Ops:
  7.2 2.9 copy.77
  11.1 4.7 %gather_fusion.6 = s32[512]{0:T(512)S(1)} fusion(s32[2,14]{1,0:T(2,128)S(1)} %copy-done, s32[512]{0:T(512)S(1)} %bitcast.125), kind=kCustom, calls=%fused_computation.6 | custom fusion | bytes 8192 | tf_op jit(solution)/shard_map/jit(take_along_axis)/gather | solution.py:96
  15.9 5.5 %scatter_fusion = bf16[3584,256]{1,0:T(8,128)(2,1)} fusion(bf16[3584,256]{1,0:T(8,128)(2,1)} %bitcast.130, s32[512]{0:T(512)S(1)} %bitcast.143, bf16[512,256]{1,0:T(8,128)(2,1)S(1)} %copy-done.7), kind=kCustom, calls=%fused_computation.7 | custom fusion | bytes 788480 | tf_op jit(solution)/shard_map/scatter | solution.py:103
  21.4 3.5 gather_fusion.3
  25.0 3.6 scatter_fusion.1
  28.5 1.6 gather_fusion.4
  30.1 3.1 gather_fusion.1
  33.2 1.5 gather_fusion.2
  34.7 2.7 fusion.68
  37.4 2.4 copy.45
  40.0 1.1 copy.35
  41.7 1.0 copy.36
  42.8 1.3 copy.44
  44.1 2.2 reshape.720
  46.7 1.1 copy.31
  48.2 66.8 %while.21 = (s32[]{:T(128)}, bf16[8,256,2,128]{1,3,0,2:T(8,128)(2,1)S(1)}, s32[1,256]{1,0:T(1,128)S(1)}, bf16[8,256,2,128]{1,3,0,2:T(8,128)(2,1)}, bf16[1792,2,1...) while((s32[]{:T(128)}, bf16[8,256,2,128]{1,3,0,2:T(8,128)(2,1)S(1)}, ...), condition=%wide.region_13.14_spmd, body=%wide.region_10.13_spmd.sunk | while | flops 476710656 | bytes 11342941 | solution.py:123
  48.5 4.6 %fusion.93 = (f32[2,256]{1,0:T(2,128)S(1)}, f32[2,256,1792]{2,1,0:T(8,128)}) fusion(bf16[1792,2,128]{2,0,1:T(8,128)(2,1)S(1)} %get-tuple-element.251, pred[256,1792]{1,0:T(8,128)(4,1)S(1)} %iota_compare_fusion.6, bf16[8,256,2,128]{1,3,0,2:T(8,128)(2,1)} %get-tuple-element.250, s32[]{:T(128)S(6)} %copy.63), kind=kOutput, calls=%fused_computation.132.clone.1 | convolution fusion | flops 239470336 | bytes 5638148 | tf_op jit(solution)/shard_map/while/body/eval_jaxpr/sub | solution.py:20
  53.1 3.0 fusion.94
  56.6 4.6 %fusion.93 = (f32[2,256]{1,0:T(2,128)S(1)}, f32[2,256,1792]{2,1,0:T(8,128)}) fusion(bf16[1792,2,128]{2,0,1:T(8,128)(2,1)S(1)} %get-tuple-element.251, pred[256,1792]{1,0:T(8,128)(4,1)S(1)} %iota_compare_fusion.6, bf16[8,256,2,128]{1,3,0,2:T(8,128)(2,1)} %get-tuple-element.250, s32[]{:T(128)S(6)} %copy.63), kind=kOutput, calls=%fused_computation.132.clone.1 | convolution fusion | flops 239470336 | bytes 5638148 | tf_op jit(solution)/shard_map/while/body/eval_jaxpr/sub | solution.py:20
  61.3 3.0 fusion.94
  64.7 4.6 %fusion.93 = (f32[2,256]{1,0:T(2,128)S(1)}, f32[2,256,1792]{2,1,0:T(8,128)}) fusion(bf16[1792,2,128]{2,0,1:T(8,128)(2,1)S(1)} %get-tuple-element.251, pred[256,1792]{1,0:T(8,128)(4,1)S(1)} %iota_compare_fusion.6, bf16[8,256,2,128]{1,3,0,2:T(8,128)(2,1)} %get-tuple-element.250, s32[]{:T(128)S(6)} %copy.63), kind=kOutput, calls=%fused_computation.132.clone.1 | convolution fusion | flops 239470336 | bytes 5638148 | tf_op jit(solution)/shard_map/while/body/eval_jaxpr/sub | solution.py:20
  69.4 3.0 fusion.94
  72.8 4.6 %fusion.93 = (f32[2,256]{1,0:T(2,128)S(1)}, f32[2,256,1792]{2,1,0:T(8,128)}) fusion(bf16[1792,2,128]{2,0,1:T(8,128)(2,1)S(1)} %get-tuple-element.251, pred[256,1792]{1,0:T(8,128)(4,1)S(1)} %iota_compare_fusion.6, bf16[8,256,2,128]{1,3,0,2:T(8,128)(2,1)} %get-tuple-element.250, s32[]{:T(128)S(6)} %copy.63), kind=kOutput, calls=%fused_computation.132.clone.1 | convolution fusion | flops 239470336 | bytes 5638148 | tf_op jit(solution)/shard_map/while/body/eval_jaxpr/sub | solution.py:20
  77.5 4.4 %fusion.94 = bf16[1,256,2,128]{3,1,2,0:T(8,128)(2,1)S(1)} fusion(bf16[1792,2,128]{2,0,1:T(8,128)(2,1)} %get-tuple-element.252, f32[2,256,1792]{2,1,0:T(8,128)} %get-tuple-element.231, f32[2,256]{1,0:T(2,128)S(1)} %get-tuple-element.232), kind=kOutput, calls=%fused_computation.37.clone.1 | convolution fusion | flops 236781568 | bytes 4720640 | tf_op jit(solution)/shard_map/while/body/eval_jaxpr/kts,skd->tkd/dot_general | solution.py:22
  82.3 4.7 %fusion.93 = (f32[2,256]{1,0:T(2,128)S(1)}, f32[2,256,1792]{2,1,0:T(8,128)}) fusion(bf16[1792,2,128]{2,0,1:T(8,128)(2,1)S(1)} %get-tuple-element.251, pred[256,1792]{1,0:T(8,128)(4,1)S(1)} %iota_compare_fusion.6, bf16[8,256,2,128]{1,3,0,2:T(8,128)(2,1)} %get-tuple-element.250, s32[]{:T(128)S(6)} %copy.63), kind=kOutput, calls=%fused_computation.132.clone.1 | convolution fusion | flops 239470336 | bytes 5638148 | tf_op jit(solution)/shard_map/while/body/eval_jaxpr/sub | solution.py:20
  87.0 3.0 fusion.94
  90.5 4.6 %fusion.93 = (f32[2,256]{1,0:T(2,128)S(1)}, f32[2,256,1792]{2,1,0:T(8,128)}) fusion(bf16[1792,2,128]{2,0,1:T(8,128)(2,1)S(1)} %get-tuple-element.251, pred[256,1792]{1,0:T(8,128)(4,1)S(1)} %iota_compare_fusion.6, bf16[8,256,2,128]{1,3,0,2:T(8,128)(2,1)} %get-tuple-element.250, s32[]{:T(128)S(6)} %copy.63), kind=kOutput, calls=%fused_computation.132.clone.1 | convolution fusion | flops 239470336 | bytes 5638148 | tf_op jit(solution)/shard_map/while/body/eval_jaxpr/sub | solution.py:20
  95.1 3.0 fusion.94
  98.6 4.6 %fusion.93 = (f32[2,256]{1,0:T(2,128)S(1)}, f32[2,256,1792]{2,1,0:T(8,128)}) fusion(bf16[1792,2,128]{2,0,1:T(8,128)(2,1)S(1)} %get-tuple-element.251, pred[256,1792]{1,0:T(8,128)(4,1)S(1)} %iota_compare_fusion.6, bf16[8,256,2,128]{1,3,0,2:T(8,128)(2,1)} %get-tuple-element.250, s32[]{:T(128)S(6)} %copy.63), kind=kOutput, calls=%fused_computation.132.clone.1 | convolution fusion | flops 239470336 | bytes 5638148 | tf_op jit(solution)/shard_map/while/body/eval_jaxpr/sub | solution.py:20
  103.2 3.5 fusion.94
  107.2 4.6 %fusion.93 = (f32[2,256]{1,0:T(2,128)S(1)}, f32[2,256,1792]{2,1,0:T(8,128)}) fusion(bf16[1792,2,128]{2,0,1:T(8,128)(2,1)S(1)} %get-tuple-element.251, pred[256,1792]{1,0:T(8,128)(4,1)S(1)} %iota_compare_fusion.6, bf16[8,256,2,128]{1,3,0,2:T(8,128)(2,1)} %get-tuple-element.250, s32[]{:T(128)S(6)} %copy.63), kind=kOutput, calls=%fused_computation.132.clone.1 | convolution fusion | flops 239470336 | bytes 5638148 | tf_op jit(solution)/shard_map/while/body/eval_jaxpr/sub | solution.py:20
  111.9 3.0 fusion.94
  115.1 65.1 %while.20 = (s32[]{:T(128)}, bf16[8,256,2,128]{1,3,0,2:T(8,128)(2,1)S(1)}, s32[1,256]{1,0:T(1,128)S(1)}, bf16[8,256,2,128]{1,3,0,2:T(8,128)(2,1)}, bf16[1792,2,1...) while((s32[]{:T(128)}, bf16[8,256,2,128]{1,3,0,2:T(8,128)(2,1)S(1)}, ...), condition=%wide.region_9.10_spmd, body=%wide.region_6.9_spmd.sunk | while | flops 476710656 | bytes 11342941 | solution.py:123
  115.5 4.6 %fusion.88 = (f32[2,256]{1,0:T(2,128)S(1)}, f32[2,256,1792]{2,1,0:T(8,128)}) fusion(bf16[1792,2,128]{2,0,1:T(8,128)(2,1)S(1)} %get-tuple-element.272, pred[256,1792]{1,0:T(8,128)(4,1)S(1)} %iota_compare_fusion.5, bf16[8,256,2,128]{1,3,0,2:T(8,128)(2,1)} %get-tuple-element.271, s32[]{:T(128)S(6)} %copy.69), kind=kOutput, calls=%fused_computation.131.clone.1 | convolution fusion | flops 239470336 | bytes 5638148 | tf_op jit(solution)/shard_map/while/body/eval_jaxpr/sub | solution.py:20
  120.1 3.0 fusion.89
  123.6 4.6 %fusion.88 = (f32[2,256]{1,0:T(2,128)S(1)}, f32[2,256,1792]{2,1,0:T(8,128)}) fusion(bf16[1792,2,128]{2,0,1:T(8,128)(2,1)S(1)} %get-tuple-element.272, pred[256,1792]{1,0:T(8,128)(4,1)S(1)} %iota_compare_fusion.5, bf16[8,256,2,128]{1,3,0,2:T(8,128)(2,1)} %get-tuple-element.271, s32[]{:T(128)S(6)} %copy.69), kind=kOutput, calls=%fused_computation.131.clone.1 | convolution fusion | flops 239470336 | bytes 5638148 | tf_op jit(solution)/shard_map/while/body/eval_jaxpr/sub | solution.py:20
  128.2 3.0 fusion.89
  131.7 4.6 %fusion.88 = (f32[2,256]{1,0:T(2,128)S(1)}, f32[2,256,1792]{2,1,0:T(8,128)}) fusion(bf16[1792,2,128]{2,0,1:T(8,128)(2,1)S(1)} %get-tuple-element.272, pred[256,1792]{1,0:T(8,128)(4,1)S(1)} %iota_compare_fusion.5, bf16[8,256,2,128]{1,3,0,2:T(8,128)(2,1)} %get-tuple-element.271, s32[]{:T(128)S(6)} %copy.69), kind=kOutput, calls=%fused_computation.131.clone.1 | convolution fusion | flops 239470336 | bytes 5638148 | tf_op jit(solution)/shard_map/while/body/eval_jaxpr/sub | solution.py:20
  136.3 3.2 fusion.89
  140.0 4.6 %fusion.88 = (f32[2,256]{1,0:T(2,128)S(1)}, f32[2,256,1792]{2,1,0:T(8,128)}) fusion(bf16[1792,2,128]{2,0,1:T(8,128)(2,1)S(1)} %get-tuple-element.272, pred[256,1792]{1,0:T(8,128)(4,1)S(1)} %iota_compare_fusion.5, bf16[8,256,2,128]{1,3,0,2:T(8,128)(2,1)} %get-tuple-element.271, s32[]{:T(128)S(6)} %copy.69), kind=kOutput, calls=%fused_computation.131.clone.1 | convolution fusion | flops 239470336 | bytes 5638148 | tf_op jit(solution)/shard_map/while/body/eval_jaxpr/sub | solution.py:20
  144.6 3.0 fusion.89
  148.1 4.6 %fusion.88 = (f32[2,256]{1,0:T(2,128)S(1)}, f32[2,256,1792]{2,1,0:T(8,128)}) fusion(bf16[1792,2,128]{2,0,1:T(8,128)(2,1)S(1)} %get-tuple-element.272, pred[256,1792]{1,0:T(8,128)(4,1)S(1)} %iota_compare_fusion.5, bf16[8,256,2,128]{1,3,0,2:T(8,128)(2,1)} %get-tuple-element.271, s32[]{:T(128)S(6)} %copy.69), kind=kOutput, calls=%fused_computation.131.clone.1 | convolution fusion | flops 239470336 | bytes 5638148 | tf_op jit(solution)/shard_map/while/body/eval_jaxpr/sub | solution.py:20
  152.7 3.0 fusion.89
  156.2 4.6 %fusion.88 = (f32[2,256]{1,0:T(2,128)S(1)}, f32[2,256,1792]{2,1,0:T(8,128)}) fusion(bf16[1792,2,128]{2,0,1:T(8,128)(2,1)S(1)} %get-tuple-element.272, pred[256,1792]{1,0:T(8,128)(4,1)S(1)} %iota_compare_fusion.5, bf16[8,256,2,128]{1,3,0,2:T(8,128)(2,1)} %get-tuple-element.271, s32[]{:T(128)S(6)} %copy.69), kind=kOutput, calls=%fused_computation.131.clone.1 | convolution fusion | flops 239470336 | bytes 5638148 | tf_op jit(solution)/shard_map/while/body/eval_jaxpr/sub | solution.py:20
  160.8 3.0 fusion.89
  164.3 4.6 %fusion.88 = (f32[2,256]{1,0:T(2,128)S(1)}, f32[2,256,1792]{2,1,0:T(8,128)}) fusion(bf16[1792,2,128]{2,0,1:T(8,128)(2,1)S(1)} %get-tuple-element.272, pred[256,1792]{1,0:T(8,128)(4,1)S(1)} %iota_compare_fusion.5, bf16[8,256,2,128]{1,3,0,2:T(8,128)(2,1)} %get-tuple-element.271, s32[]{:T(128)S(6)} %copy.69), kind=kOutput, calls=%fused_computation.131.clone.1 | convolution fusion | flops 239470336 | bytes 5638148 | tf_op jit(solution)/shard_map/while/body/eval_jaxpr/sub | solution.py:20
  168.9 3.0 fusion.89
  172.4 4.6 %fusion.88 = (f32[2,256]{1,0:T(2,128)S(1)}, f32[2,256,1792]{2,1,0:T(8,128)}) fusion(bf16[1792,2,128]{2,0,1:T(8,128)(2,1)S(1)} %get-tuple-element.272, pred[256,1792]{1,0:T(8,128)(4,1)S(1)} %iota_compare_fusion.5, bf16[8,256,2,128]{1,3,0,2:T(8,128)(2,1)} %get-tuple-element.271, s32[]{:T(128)S(6)} %copy.69), kind=kOutput, calls=%fused_computation.131.clone.1 | convolution fusion | flops 239470336 | bytes 5638148 | tf_op jit(solution)/shard_map/while/body/eval_jaxpr/sub | solution.py:20
  177.0 3.0 fusion.89
  180.2 25.9 %convolution_convert_fusion = bf16[512,8192]{1,0:T(8,128)(2,1)} fusion(bf16[2048,8192]{1,0:T(8,128)(2,1)} %all-gather.2.cloned.1.call-done, bf16[256,2048]{0,1:T(8,128)(2,1)S(1)} %bitcast.138, bf16[256,2048]{0,1:T(8,128)(2,1)S(1)} %bitcast.139), kind=kOutput, calls=%fused_computation.48 | convolution fusion | flops 17188257792 | bytes 44040192 | tf_op jit(solution)/shard_map/dot_general | solution.py:57
  206.8 0.6 dynamic-slice
  208.3 0.8 dynamic-update-slice.1
  209.1 9.2 %all-reduce.2 = (s32[16]{0:T(128)S(1)}, s32[8]{0:T(128)S(1)}) all-reduce(s32[16]{0:T(128)S(1)} %dynamic-update-slice, s32[8]{0:T(128)S(1)} %dynamic-update-slice.1), channel_id=1, replica_groups=mesh['req'=8,'head'=4] {'req'}, use_global_device_ids=true, to_apply=%add | all-reduce | flops 24 | bytes 192
  218.6 0.6 dynamic_slice.25
  219.8 3.6 gather_fusion
  223.5 0.7 compare_select_fusion
  224.2 0.7 add_compare_fusion
  224.9 128.4 %reduce-scatter.2.cloned.1.call-done = bf16[512,2048]{1,0:T(8,128)(2,1)} async-done(((bf16[512,8192]{1,0:T(8,128)(2,1)}), bf16[512,2048]{1,0:T(8,128)(2,1)}) %reduce-scatter.2.cloned.1.call-update) | async-done | bytes 2097168 | tf_op jit(solution)/shard_map/reduce_scatter | solution.py:65
  353.4 6.3 %gather_fusion.5 = bf16[512,2048]{1,0:T(8,128)(2,1)S(1)} fusion(bf16[512,2048]{1,0:T(8,128)(2,1)} %reduce-scatter.2.cloned.1.call-done, s32[1024]{0:T(1024)S(1)} %pad_clamp_fusion), kind=kCustom, calls=%fused_computation.5 | custom fusion | bytes 4196352 | tf_op jit(solution)/shard_map/jit(_take)/gather | solution.py:45
  359.7 1.7 select_select_fusion
  361.4 3.6 all-to-all-start
  365.4 26.2 %all-to-all-done = bf16[8,64,2048]{2,1,0:T(8,128)(2,1)S(1)} async-done(((bf16[8,64,2048]{2,1,0:T(8,128)(2,1)}), bf16[8,64,2048]{2,1,0:T(8,128)(2,1)S(1)}, u32[]{:S(2)}, u32[]{:S(2)}) %all-to-all-start) | async-done | bytes 2097184 | tf_op jit(solution)/shard_map/all_to_all | solution.py:47
  391.6 3.8 scatter_custom_fusion.2
  395.4 2.6 add_convert_fusion
  (123 shorter events, 11.7 us)
Async XLA Ops:
  7.2 173.0 %all-gather.2.cloned.1.call-start = ((), (), s32[]{:S(2)}) async-start(), calls=%async_computation.2 | async-start | bytes 37748736 | tf_op jit(solution)/shard_map/all_gather | solution.py:59
  10.1 0.7 copy-start.9
  10.1 0.9 copy-start.10
  10.1 0.9 copy-start
  10.2 5.7 %copy-start.7 = (bf16[512,256]{1,0:T(8,128)(2,1)S(1)}, bf16[512,256]{1,0:T(8,128)(2,1)}, u32[]{:S(2)}) copy-start(bf16[512,256]{1,0:T(8,128)(2,1)} %param.16) | copy-start | bytes 786436
  10.2 343.2 %reduce-scatter.2.cloned.1.call-start = ((), (), s32[]{:S(2)}) async-start(), calls=%async_computation.3 | async-start | bytes 10485760 | tf_op jit(solution)/shard_map/reduce_scatter | solution.py:65
  15.9 9.1 %copy-start.2 = (bf16[28,128,256]{2,1,0:T(8,128)(2,1)S(1)}, bf16[28,128,256]{2,1,0:T(8,128)(2,1)}, u32[]{:S(2)}) copy-start(bf16[28,128,256]{2,1,0:T(8,128)(2,1)} %param.19) | copy-start | bytes 5505028
  15.9 9.1 %copy-start.8 = (bf16[512,256]{1,0:T(8,128)(2,1)S(1)}, bf16[512,256]{1,0:T(8,128)(2,1)}, u32[]{:S(2)}) copy-start(bf16[512,256]{1,0:T(8,128)(2,1)} %param.17) | copy-start | bytes 786436
  28.5 6.2 %copy-start.1 = (bf16[3584,256]{1,0:T(8,128)(2,1)}, bf16[3584,256]{1,0:T(8,128)(2,1)S(1)}, u32[]{:S(2)}) copy-start(bf16[3584,256]{1,0:T(8,128)(2,1)S(1)} %scatter_fusion.1) | copy-start | bytes 5505028
  37.4 2.4 copy-start.4
  40.0 1.5 copy-start.5
  44.1 2.4 copy-start.3
  46.7 1.5 copy-start.6
  206.1 0.7 copy-start.11
  361.4 30.3 %all-to-all-start = ((bf16[8,64,2048]{2,1,0:T(8,128)(2,1)}), bf16[8,64,2048]{2,1,0:T(8,128)(2,1)S(1)}, u32[]{:S(2)}, u32[]{:S(2)}) async-start(bf16[8,64,2048]{2,1,0:T(8,128)(2,1)} %select_select_fusion), calls=%async_computation.1 | async-start | bytes 4194304 | tf_op jit(solution)/shard_map/all_to_all | solution.py:47
Sparse Core Ops, SparseCore 0:
  10.3 163.3 all-gather.1
  206.3 147.0 reduce-scatter.1
where the time goes:
time: 406 us; the launch traced here: 405 us
  waiting for transfers between devices  155 us (38%)
  matrix products  150 us (37%)
  local copies, waits for them, and re-layouts  59.2 us (15%)
  between operations  15.6 us (4%)
  other arithmetic  11.8 us (3%)
  blocking collectives  9.17 us (2%)
    reduce_scatter x1, waiting for transfers between devices, head_total(): lax.psum_scatter(partial_sum.astype(jnp.bfloat16), 'head', scatter_dimens...  128 us
    sub x16, matrix products, head_attention(): expo_terms = jnp.where(allowed, jnp.exp(scores - highest), 0.0)  74.1 us
    dot_general x16, matrix products, head_attention(): jnp.einsum('kts,skd->tkd', weights, prior_values, preferred_element_type=...  49.8 us
    all_to_all x1, waiting for transfers between devices, deal(): lax.all_to_all(outgoing, 'req', split_axis=0, concat_axis=0, tiled=True)  26.2 us
    dot_general x1, matrix products, project(): jnp.dot(row_block, lax.all_gather(out_weight, 'req', axis=1, tiled=True),...  25.9 us
    unnamed x40, local copies, waits for them, and re-layouts  9.63 us
    unnamed x1, blocking collectives  9.17 us
  transfers between devices with their start and end apart: 3, of which 2 were waited for; matrix products, arithmetic and copies ran while one was open for 44% of the time, Pallas kernels for 0%

commit v1 on v0

--- a/solution.py
+++ b/solution.py
@@ -44,7 +44,15 @@
     source = jnp.where(is_live, source, 0)
     picked = jnp.take(row_block, source.reshape(-1), axis=0).reshape(groups, pair_slots, columns)
     outgoing = jnp.where(is_live[:, :, None], picked, jnp.zeros((), row_block.dtype))
-    arrived = lax.all_to_all(outgoing, "req", split_axis=0, concat_axis=0, tiled=True)
+    ways, here = (lax.axis_size("req"), lax.axis_index("req"))
+    width = outgoing.shape[0] // ways
+    turned = jnp.roll(outgoing, -here * width, axis=0)
+    got = [lax.slice_in_dim(turned, 0, width, axis=0)]
+    for far in range(1, ways):
+        sent = lax.slice_in_dim(turned, far * width, (far + 1) * width, axis=0)
+        got.append(lax.ppermute(sent, "req", [(d, (d + far) % ways) for d in range(ways)]))
+    line = jnp.concatenate(got[::-1], axis=0)
+    arrived = jnp.roll(line, (here + 1) * got[0].shape[0], axis=0)
     own_shares = lax.dynamic_index_in_dim(shares, my_rank, 1, keepdims=False)
     own_starts = lax.dynamic_index_in_dim(starts, my_rank, 1, keepdims=False)
     within = jnp.arange(pair_slots, dtype=jnp.int32)[None, :]

time: 406 us -> 420 us (1.034)
  waiting for transfers between devices: 155 us -> 165 us
    all_to_all x1 -> x0, waiting for transfers between devices: 26.2 us -> none  [deal(): lax.all_to_all(outgoing, 'req', split_axis=0, concat_axis=0, tiled=True)]
    ppermute x0 -> x7, waiting for transfers between devices: none -> 21.5 us  [deal(): lax.ppermute(sent, 'req', [(d, (d + far) % ways) for d in range(ways)])]
    reduce_scatter x1, waiting for transfers between devices: 128 us -> 144 us  [head_total(): lax.psum_scatter(partial_sum.astype(jnp.bfloat16), 'head', scatter_dimens...]
    ppermute x0 -> x7, starting transfers between devices: none -> 4.78 us  [deal(): lax.ppermute(sent, 'req', [(d, (d + far) % ways) for d in range(ways)])]
    unnamed x40 -> x47, local copies, waits for them, and re-layouts: 9.63 us -> 11.1 us
  transfers between devices with their start and end apart: 3 -> 9, of which waited for: 2 -> 5; matrix products, arithmetic and copies ran while one was open for 44% -> 42% of each run, Pallas kernels for 0% -> 0%
where the time goes in v1:
time: 420 us; the launch traced here: 419 us
  waiting for transfers between devices  165 us (39%)
  matrix products  150 us (36%)
  local copies, waits for them, and re-layouts  61.2 us (15%)
  between operations  15.8 us (4%)
  other arithmetic  11.8 us (3%)
  blocking collectives  9.49 us (2%)
  starting transfers between devices  4.86 us (1%)
    reduce_scatter x1, waiting for transfers between devices, head_total(): lax.psum_scatter(partial_sum.astype(jnp.bfloat16), 'head', scatter_dimens...  144 us
    sub x16, matrix products, head_attention(): expo_terms = jnp.where(allowed, jnp.exp(scores - highest), 0.0)  74.2 us
    dot_general x16, matrix products, head_attention(): jnp.einsum('kts,skd->tkd', weights, prior_values, preferred_element_type=...  49.7 us
    dot_general x1, matrix products, project(): jnp.dot(row_block, lax.all_gather(out_weight, 'req', axis=1, tiled=True),...  25.9 us
    ppermute x7, waiting for transfers between devices, deal(): lax.ppermute(sent, 'req', [(d, (d + far) % ways) for d in range(ways)])  21.5 us
    unnamed x47, local copies, waits for them, and re-layouts  11.1 us
    unnamed x1, blocking collectives  9.49 us
  transfers between devices with their start and end apart: 9, of which 5 were waited for; matrix products, arithmetic and copies ran while one was open for 42% of the time, Pallas kernels for 0%

profile of v1, /device:TPU:0, one launch (start us, length us, event | category | flops | bytes accessed | tf_op | source)
XLA Modules:
  0.0 418.7 jit_solution(16438353246714492377)
XLA Ops:
  7.2 2.9 copy.84
  13.1 9.5 %all-reduce.2 = (s32[16]{0:T(128)S(1)}, s32[8]{0:T(128)S(1)}) all-reduce(s32[16]{0:T(128)S(1)} %dynamic-update-slice, s32[8]{0:T(128)S(1)} %dynamic-update-slice.1), channel_id=1, replica_groups=mesh['req'=8,'head'=4] {'req'}, use_global_device_ids=true, to_apply=%add | all-reduce | flops 24 | bytes 192
  24.5 3.3 gather_fusion
  27.9 4.8 %gather_fusion.6 = s32[512]{0:T(512)S(1)} fusion(s32[2,14]{1,0:T(2,128)S(1)} %copy-done, s32[512]{0:T(512)S(1)} %bitcast.125), kind=kCustom, calls=%fused_computation.6 | custom fusion | bytes 8192 | tf_op jit(solution)/shard_map/jit(take_along_axis)/gather | solution.py:104
  33.3 5.5 %scatter_fusion = bf16[3584,256]{1,0:T(8,128)(2,1)} fusion(bf16[3584,256]{1,0:T(8,128)(2,1)} %bitcast.130, s32[512]{0:T(512)S(1)} %bitcast.143, bf16[512,256]{1,0:T(8,128)(2,1)S(1)} %copy-done.7), kind=kCustom, calls=%fused_computation.7 | custom fusion | bytes 788480 | tf_op jit(solution)/shard_map/scatter | solution.py:111
  38.8 3.1 gather_fusion.3
  41.9 3.6 scatter_fusion.1
  45.4 1.6 gather_fusion.4
  47.0 3.1 gather_fusion.1
  50.1 1.5 gather_fusion.2
  51.6 2.7 fusion.71
  54.3 2.4 copy.45
  56.9 1.1 copy.35
  58.6 1.0 copy.36
  59.6 1.3 copy.44
  60.9 2.2 reshape.720
  63.6 1.1 copy.31
  65.1 66.5 %while.21 = (s32[]{:T(128)}, bf16[8,256,2,128]{1,3,0,2:T(8,128)(2,1)S(1)}, s32[1,256]{1,0:T(1,128)S(1)}, bf16[8,256,2,128]{1,3,0,2:T(8,128)(2,1)}, bf16[1792,2,1...) while((s32[]{:T(128)}, bf16[8,256,2,128]{1,3,0,2:T(8,128)(2,1)S(1)}, ...), condition=%wide.region_13.14_spmd, body=%wide.region_10.13_spmd.sunk | while | flops 476710656 | bytes 11342941 | solution.py:131
  65.4 4.6 %fusion.96 = (f32[2,256]{1,0:T(2,128)S(1)}, f32[2,256,1792]{2,1,0:T(8,128)}) fusion(bf16[1792,2,128]{2,0,1:T(8,128)(2,1)S(1)} %get-tuple-element.261, pred[256,1792]{1,0:T(8,128)(4,1)S(1)} %iota_compare_fusion.6, bf16[8,256,2,128]{1,3,0,2:T(8,128)(2,1)} %get-tuple-element.260, s32[]{:T(128)S(6)} %copy.63), kind=kOutput, calls=%fused_computation.146.clone.1 | convolution fusion | flops 239470336 | bytes 5638148 | tf_op jit(solution)/shard_map/while/body/eval_jaxpr/sub | solution.py:20
  70.0 3.0 fusion.97
  73.5 4.6 %fusion.96 = (f32[2,256]{1,0:T(2,128)S(1)}, f32[2,256,1792]{2,1,0:T(8,128)}) fusion(bf16[1792,2,128]{2,0,1:T(8,128)(2,1)S(1)} %get-tuple-element.261, pred[256,1792]{1,0:T(8,128)(4,1)S(1)} %iota_compare_fusion.6, bf16[8,256,2,128]{1,3,0,2:T(8,128)(2,1)} %get-tuple-element.260, s32[]{:T(128)S(6)} %copy.63), kind=kOutput, calls=%fused_computation.146.clone.1 | convolution fusion | flops 239470336 | bytes 5638148 | tf_op jit(solution)/shard_map/while/body/eval_jaxpr/sub | solution.py:20
  78.1 4.4 %fusion.97 = bf16[1,256,2,128]{3,1,2,0:T(8,128)(2,1)S(1)} fusion(bf16[1792,2,128]{2,0,1:T(8,128)(2,1)} %get-tuple-element.262, f32[2,256,1792]{2,1,0:T(8,128)} %get-tuple-element.241, f32[2,256]{1,0:T(2,128)S(1)} %get-tuple-element.242), kind=kOutput, calls=%fused_computation.37.clone.1 | convolution fusion | flops 236781568 | bytes 4720640 | tf_op jit(solution)/shard_map/while/body/eval_jaxpr/kts,skd->tkd/dot_general | solution.py:22
  83.0 4.7 %fusion.96 = (f32[2,256]{1,0:T(2,128)S(1)}, f32[2,256,1792]{2,1,0:T(8,128)}) fusion(bf16[1792,2,128]{2,0,1:T(8,128)(2,1)S(1)} %get-tuple-element.261, pred[256,1792]{1,0:T(8,128)(4,1)S(1)} %iota_compare_fusion.6, bf16[8,256,2,128]{1,3,0,2:T(8,128)(2,1)} %get-tuple-element.260, s32[]{:T(128)S(6)} %copy.63), kind=kOutput, calls=%fused_computation.146.clone.1 | convolution fusion | flops 239470336 | bytes 5638148 | tf_op jit(solution)/shard_map/while/body/eval_jaxpr/sub | solution.py:20
  87.7 3.0 fusion.97
  91.2 4.6 %fusion.96 = (f32[2,256]{1,0:T(2,128)S(1)}, f32[2,256,1792]{2,1,0:T(8,128)}) fusion(bf16[1792,2,128]{2,0,1:T(8,128)(2,1)S(1)} %get-tuple-element.261, pred[256,1792]{1,0:T(8,128)(4,1)S(1)} %iota_compare_fusion.6, bf16[8,256,2,128]{1,3,0,2:T(8,128)(2,1)} %get-tuple-element.260, s32[]{:T(128)S(6)} %copy.63), kind=kOutput, calls=%fused_computation.146.clone.1 | convolution fusion | flops 239470336 | bytes 5638148 | tf_op jit(solution)/shard_map/while/body/eval_jaxpr/sub | solution.py:20
  95.8 3.0 fusion.97
  99.3 4.6 %fusion.96 = (f32[2,256]{1,0:T(2,128)S(1)}, f32[2,256,1792]{2,1,0:T(8,128)}) fusion(bf16[1792,2,128]{2,0,1:T(8,128)(2,1)S(1)} %get-tuple-element.261, pred[256,1792]{1,0:T(8,128)(4,1)S(1)} %iota_compare_fusion.6, bf16[8,256,2,128]{1,3,0,2:T(8,128)(2,1)} %get-tuple-element.260, s32[]{:T(128)S(6)} %copy.63), kind=kOutput, calls=%fused_computation.146.clone.1 | convolution fusion | flops 239470336 | bytes 5638148 | tf_op jit(solution)/shard_map/while/body/eval_jaxpr/sub | solution.py:20
  103.9 3.1 fusion.97
  107.5 4.6 %fusion.96 = (f32[2,256]{1,0:T(2,128)S(1)}, f32[2,256,1792]{2,1,0:T(8,128)}) fusion(bf16[1792,2,128]{2,0,1:T(8,128)(2,1)S(1)} %get-tuple-element.261, pred[256,1792]{1,0:T(8,128)(4,1)S(1)} %iota_compare_fusion.6, bf16[8,256,2,128]{1,3,0,2:T(8,128)(2,1)} %get-tuple-element.260, s32[]{:T(128)S(6)} %copy.63), kind=kOutput, calls=%fused_computation.146.clone.1 | convolution fusion | flops 239470336 | bytes 5638148 | tf_op jit(solution)/shard_map/while/body/eval_jaxpr/sub | solution.py:20
  112.2 3.0 fusion.97
  115.6 4.6 %fusion.96 = (f32[2,256]{1,0:T(2,128)S(1)}, f32[2,256,1792]{2,1,0:T(8,128)}) fusion(bf16[1792,2,128]{2,0,1:T(8,128)(2,1)S(1)} %get-tuple-element.261, pred[256,1792]{1,0:T(8,128)(4,1)S(1)} %iota_compare_fusion.6, bf16[8,256,2,128]{1,3,0,2:T(8,128)(2,1)} %get-tuple-element.260, s32[]{:T(128)S(6)} %copy.63), kind=kOutput, calls=%fused_computation.146.clone.1 | convolution fusion | flops 239470336 | bytes 5638148 | tf_op jit(solution)/shard_map/while/body/eval_jaxpr/sub | solution.py:20
  120.3 3.0 fusion.97
  123.8 4.6 %fusion.96 = (f32[2,256]{1,0:T(2,128)S(1)}, f32[2,256,1792]{2,1,0:T(8,128)}) fusion(bf16[1792,2,128]{2,0,1:T(8,128)(2,1)S(1)} %get-tuple-element.261, pred[256,1792]{1,0:T(8,128)(4,1)S(1)} %iota_compare_fusion.6, bf16[8,256,2,128]{1,3,0,2:T(8,128)(2,1)} %get-tuple-element.260, s32[]{:T(128)S(6)} %copy.63), kind=kOutput, calls=%fused_computation.146.clone.1 | convolution fusion | flops 239470336 | bytes 5638148 | tf_op jit(solution)/shard_map/while/body/eval_jaxpr/sub | solution.py:20
  128.4 3.0 fusion.97
  131.6 65.3 %while.20 = (s32[]{:T(128)}, bf16[8,256,2,128]{1,3,0,2:T(8,128)(2,1)S(1)}, s32[1,256]{1,0:T(1,128)S(1)}, bf16[8,256,2,128]{1,3,0,2:T(8,128)(2,1)}, bf16[1792,2,1...) while((s32[]{:T(128)}, bf16[8,256,2,128]{1,3,0,2:T(8,128)(2,1)S(1)}, ...), condition=%wide.region_9.10_spmd, body=%wide.region_6.9_spmd.sunk | while | flops 476710656 | bytes 11342941 | solution.py:131
  132.0 4.6 %fusion.91 = (f32[2,256]{1,0:T(2,128)S(1)}, f32[2,256,1792]{2,1,0:T(8,128)}) fusion(bf16[1792,2,128]{2,0,1:T(8,128)(2,1)S(1)} %get-tuple-element.282, pred[256,1792]{1,0:T(8,128)(4,1)S(1)} %iota_compare_fusion.5, bf16[8,256,2,128]{1,3,0,2:T(8,128)(2,1)} %get-tuple-element.281, s32[]{:T(128)S(6)} %copy.69), kind=kOutput, calls=%fused_computation.145.clone.1 | convolution fusion | flops 239470336 | bytes 5638148 | tf_op jit(solution)/shard_map/while/body/eval_jaxpr/sub | solution.py:20
  136.6 3.2 fusion.92
  140.3 4.6 %fusion.91 = (f32[2,256]{1,0:T(2,128)S(1)}, f32[2,256,1792]{2,1,0:T(8,128)}) fusion(bf16[1792,2,128]{2,0,1:T(8,128)(2,1)S(1)} %get-tuple-element.282, pred[256,1792]{1,0:T(8,128)(4,1)S(1)} %iota_compare_fusion.5, bf16[8,256,2,128]{1,3,0,2:T(8,128)(2,1)} %get-tuple-element.281, s32[]{:T(128)S(6)} %copy.69), kind=kOutput, calls=%fused_computation.145.clone.1 | convolution fusion | flops 239470336 | bytes 5638148 | tf_op jit(solution)/shard_map/while/body/eval_jaxpr/sub | solution.py:20
  144.9 3.0 fusion.92
  148.4 4.7 %fusion.91 = (f32[2,256]{1,0:T(2,128)S(1)}, f32[2,256,1792]{2,1,0:T(8,128)}) fusion(bf16[1792,2,128]{2,0,1:T(8,128)(2,1)S(1)} %get-tuple-element.282, pred[256,1792]{1,0:T(8,128)(4,1)S(1)} %iota_compare_fusion.5, bf16[8,256,2,128]{1,3,0,2:T(8,128)(2,1)} %get-tuple-element.281, s32[]{:T(128)S(6)} %copy.69), kind=kOutput, calls=%fused_computation.145.clone.1 | convolution fusion | flops 239470336 | bytes 5638148 | tf_op jit(solution)/shard_map/while/body/eval_jaxpr/sub | solution.py:20
  153.1 3.0 fusion.92
  156.6 4.6 %fusion.91 = (f32[2,256]{1,0:T(2,128)S(1)}, f32[2,256,1792]{2,1,0:T(8,128)}) fusion(bf16[1792,2,128]{2,0,1:T(8,128)(2,1)S(1)} %get-tuple-element.282, pred[256,1792]{1,0:T(8,128)(4,1)S(1)} %iota_compare_fusion.5, bf16[8,256,2,128]{1,3,0,2:T(8,128)(2,1)} %get-tuple-element.281, s32[]{:T(128)S(6)} %copy.69), kind=kOutput, calls=%fused_computation.145.clone.1 | convolution fusion | flops 239470336 | bytes 5638148 | tf_op jit(solution)/shard_map/while/body/eval_jaxpr/sub | solution.py:20
  161.2 3.0 fusion.92
  164.7 4.6 %fusion.91 = (f32[2,256]{1,0:T(2,128)S(1)}, f32[2,256,1792]{2,1,0:T(8,128)}) fusion(bf16[1792,2,128]{2,0,1:T(8,128)(2,1)S(1)} %get-tuple-element.282, pred[256,1792]{1,0:T(8,128)(4,1)S(1)} %iota_compare_fusion.5, bf16[8,256,2,128]{1,3,0,2:T(8,128)(2,1)} %get-tuple-element.281, s32[]{:T(128)S(6)} %copy.69), kind=kOutput, calls=%fused_computation.145.clone.1 | convolution fusion | flops 239470336 | bytes 5638148 | tf_op jit(solution)/shard_map/while/body/eval_jaxpr/sub | solution.py:20
  169.3 3.2 fusion.92
  173.0 4.6 %fusion.91 = (f32[2,256]{1,0:T(2,128)S(1)}, f32[2,256,1792]{2,1,0:T(8,128)}) fusion(bf16[1792,2,128]{2,0,1:T(8,128)(2,1)S(1)} %get-tuple-element.282, pred[256,1792]{1,0:T(8,128)(4,1)S(1)} %iota_compare_fusion.5, bf16[8,256,2,128]{1,3,0,2:T(8,128)(2,1)} %get-tuple-element.281, s32[]{:T(128)S(6)} %copy.69), kind=kOutput, calls=%fused_computation.145.clone.1 | convolution fusion | flops 239470336 | bytes 5638148 | tf_op jit(solution)/shard_map/while/body/eval_jaxpr/sub | solution.py:20
  177.6 3.0 fusion.92
  181.1 4.6 %fusion.91 = (f32[2,256]{1,0:T(2,128)S(1)}, f32[2,256,1792]{2,1,0:T(8,128)}) fusion(bf16[1792,2,128]{2,0,1:T(8,128)(2,1)S(1)} %get-tuple-element.282, pred[256,1792]{1,0:T(8,128)(4,1)S(1)} %iota_compare_fusion.5, bf16[8,256,2,128]{1,3,0,2:T(8,128)(2,1)} %get-tuple-element.281, s32[]{:T(128)S(6)} %copy.69), kind=kOutput, calls=%fused_computation.145.clone.1 | convolution fusion | flops 239470336 | bytes 5638148 | tf_op jit(solution)/shard_map/while/body/eval_jaxpr/sub | solution.py:20
  185.7 3.0 fusion.92
  189.2 4.6 %fusion.91 = (f32[2,256]{1,0:T(2,128)S(1)}, f32[2,256,1792]{2,1,0:T(8,128)}) fusion(bf16[1792,2,128]{2,0,1:T(8,128)(2,1)S(1)} %get-tuple-element.282, pred[256,1792]{1,0:T(8,128)(4,1)S(1)} %iota_compare_fusion.5, bf16[8,256,2,128]{1,3,0,2:T(8,128)(2,1)} %get-tuple-element.281, s32[]{:T(128)S(6)} %copy.69), kind=kOutput, calls=%fused_computation.145.clone.1 | convolution fusion | flops 239470336 | bytes 5638148 | tf_op jit(solution)/shard_map/while/body/eval_jaxpr/sub | solution.py:20
  193.8 3.0 fusion.92
  197.0 25.9 %convolution_convert_fusion = bf16[512,8192]{1,0:T(8,128)(2,1)} fusion(bf16[2048,8192]{1,0:T(8,128)(2,1)} %all-gather.2.cloned.1.call-done, bf16[256,2048]{0,1:T(8,128)(2,1)S(1)} %bitcast.138, bf16[256,2048]{0,1:T(8,128)(2,1)S(1)} %bitcast.139), kind=kOutput, calls=%fused_computation.48 | convolution fusion | flops 17188257792 | bytes 44040192 | tf_op jit(solution)/shard_map/dot_general | solution.py:65
  223.9 143.6 %reduce-scatter.2.cloned.1.call-done = bf16[512,2048]{1,0:T(8,128)(2,1)} async-done(((bf16[512,8192]{1,0:T(8,128)(2,1)}), bf16[512,2048]{1,0:T(8,128)(2,1)}) %reduce-scatter.2.cloned.1.call-update) | async-done | bytes 2097168 | tf_op jit(solution)/shard_map/reduce_scatter | solution.py:73
  367.5 6.5 %gather_fusion.5 = bf16[512,2048]{1,0:T(8,128)(2,1)S(1)} fusion(bf16[512,2048]{1,0:T(8,128)(2,1)} %reduce-scatter.2.cloned.1.call-done, s32[1024]{0:T(1024)S(1)} %pad_clamp_fusion), kind=kCustom, calls=%fused_computation.5 | custom fusion | bytes 4196352 | tf_op jit(solution)/shard_map/jit(_take)/gather | solution.py:45
  375.2 1.0 fusion.70
  376.1 1.4 collective-permute-start
  379.0 1.5 collective-permute-start.3
  380.7 3.3 collective-permute-done
  384.4 1.0 constant_dynamic-update-slice_fusion.8
  385.3 5.1 %collective-permute-done.1 = bf16[1,64,2048]{2,1,0:T(8,128)(2,1)} collective-permute-done((bf16[1,64,2048]{2,1,0:T(8,128)(2,1)}, bf16[1,64,2048]{2,1,0:T(8,128)(2,1)}, u32[]{:S(2)}, u32[]{:S(2)}) %collective-permute-start.1) | collective-permute-done | bytes 262176 | tf_op jit(solution)/shard_map/ppermute | solution.py:53
  390.4 1.0 constant_dynamic-update-slice_fusion.7
  391.4 12.8 %collective-permute-done.3 = bf16[1,64,2048]{2,1,0:T(8,128)(2,1)S(1)} collective-permute-done((bf16[1,64,2048]{2,1,0:T(8,128)(2,1)S(1)}, bf16[1,64,2048]{2,1,0:T(8,128)(2,1)S(1)}, u32[]{:S(2)}, u32[]{:S(2)}) %collective-permute-start.3) | collective-permute-done | bytes 262176 | tf_op jit(solution)/shard_map/ppermute | solution.py:53
  405.4 3.8 scatter_custom_fusion.2
  409.2 2.6 add_convert_fusion
  (145 shorter events, 18.4 us)
Async XLA Ops:
  7.2 189.8 %all-gather.2.cloned.1.call-start = ((), (), s32[]{:S(2)}) async-start(), calls=%async_computation.1 | async-start | bytes 37748736 | tf_op jit(solution)/shard_map/all_gather | solution.py:67
  10.1 0.7 copy-start.11
  10.1 2.0 copy-start.10
  10.1 14.0 %copy-start.9 = (s32[2]{0:T(128)S(1)}, s32[2]{0:T(128)}, u32[]{:S(2)}) copy-start(s32[2]{0:T(128)} %param.24) | copy-start | bytes 28
  10.2 357.4 %reduce-scatter.2.cloned.1.call-start = ((), (), s32[]{:S(2)}) async-start(), calls=%async_computation.2 | async-start | bytes 10485760 | tf_op jit(solution)/shard_map/reduce_scatter | solution.py:73
  24.5 3.4 copy-start
  27.9 5.4 %copy-start.7 = (bf16[512,256]{1,0:T(8,128)(2,1)S(1)}, bf16[512,256]{1,0:T(8,128)(2,1)}, u32[]{:S(2)}) copy-start(bf16[512,256]{1,0:T(8,128)(2,1)} %param.18) | copy-start | bytes 786436
  33.2 8.6 %copy-start.2 = (bf16[28,128,256]{2,1,0:T(8,128)(2,1)S(1)}, bf16[28,128,256]{2,1,0:T(8,128)(2,1)}, u32[]{:S(2)}) copy-start(bf16[28,128,256]{2,1,0:T(8,128)(2,1)} %param.21) | copy-start | bytes 5505028
  33.3 8.6 %copy-start.8 = (bf16[512,256]{1,0:T(8,128)(2,1)S(1)}, bf16[512,256]{1,0:T(8,128)(2,1)}, u32[]{:S(2)}) copy-start(bf16[512,256]{1,0:T(8,128)(2,1)} %param.19) | copy-start | bytes 786436
  45.4 6.2 %copy-start.1 = (bf16[3584,256]{1,0:T(8,128)(2,1)}, bf16[3584,256]{1,0:T(8,128)(2,1)S(1)}, u32[]{:S(2)}) copy-start(bf16[3584,256]{1,0:T(8,128)(2,1)S(1)} %scatter_fusion.1) | copy-start | bytes 5505028
  54.3 2.4 copy-start.4
  56.9 1.5 copy-start.5
  60.9 2.4 copy-start.3
  63.6 1.5 copy-start.6
  376.1 7.8 %collective-permute-start = (bf16[1,64,2048]{2,1,0:T(8,128)(2,1)}, bf16[1,64,2048]{2,1,0:T(8,128)(2,1)}, u32[]{:S(2)}, u32[]{:S(2)}) collective-permute-start(bf16[1,64,2048]{2,1,0:T(8,128)(2,1)} %get-tuple-element.142), channel_id=1, source_target_pairs={{0,28},{4,0},{8,4},{12,8},{16,12},{20,16},{24,20},{28,24},{1,29},{... | collective-permute-start | bytes 786440 | tf_op jit(solution)/shard_map/ppermute | solution.py:53
  377.7 12.7 %collective-permute-start.1 = (bf16[1,64,2048]{2,1,0:T(8,128)(2,1)}, bf16[1,64,2048]{2,1,0:T(8,128)(2,1)}, u32[]{:S(2)}, u32[]{:S(2)}) collective-permute-start(bf16[1,64,2048]{2,1,0:T(8,128)(2,1)} %get-tuple-element.141), channel_id=1, source_target_pairs={{0,24},{4,28},{8,0},{12,4},{16,8},{20,12},{24,16},{28,20},{1,25},{... | collective-permute-start | bytes 786440 | tf_op jit(solution)/shard_map/ppermute | solution.py:53
  378.7 12.7 %collective-permute-start.2 = (bf16[1,64,2048]{2,1,0:T(8,128)(2,1)S(1)}, bf16[1,64,2048]{2,1,0:T(8,128)(2,1)S(1)}, u32[]{:S(2)}, u32[]{:S(2)}) collective-permute-start(bf16[1,64,2048]{2,1,0:T(8,128)(2,1)S(1)} %get-tuple-element.140), channel_id=1, source_target_pairs={{0,20},{4,24},{8,28},{12,0},{16,4},{20,8},{24,12},{28,16},{1,21},{... | collective-permute-start | bytes 786440 | tf_op jit(solution)/shard_map/ppermute | solution.py:53
  379.0 25.1 %collective-permute-start.3 = (bf16[1,64,2048]{2,1,0:T(8,128)(2,1)S(1)}, bf16[1,64,2048]{2,1,0:T(8,128)(2,1)S(1)}, u32[]{:S(2)}, u32[]{:S(2)}) collective-permute-start(bf16[1,64,2048]{2,1,0:T(8,128)(2,1)S(1)} %get-tuple-element.139), channel_id=1, source_target_pairs={{0,16},{4,20},{8,24},{12,28},{16,0},{20,4},{24,8},{28,12},{1,17},{... | collective-permute-start | bytes 786440 | tf_op jit(solution)/shard_map/ppermute | solution.py:53
  380.5 24.0 %collective-permute-start.4 = (bf16[1,64,2048]{2,1,0:T(8,128)(2,1)S(1)}, bf16[1,64,2048]{2,1,0:T(8,128)(2,1)S(1)}, u32[]{:S(2)}, u32[]{:S(2)}) collective-permute-start(bf16[1,64,2048]{2,1,0:T(8,128)(2,1)S(1)} %get-tuple-element.138), channel_id=1, source_target_pairs={{0,12},{4,16},{8,20},{12,24},{16,28},{20,0},{24,4},{28,8},{1,13},{... | collective-permute-start | bytes 786440 | tf_op jit(solution)/shard_map/ppermute | solution.py:53
  384.0 20.6 %collective-permute-start.5 = (bf16[1,64,2048]{2,1,0:T(8,128)(2,1)S(1)}, bf16[1,64,2048]{2,1,0:T(8,128)(2,1)S(1)}, u32[]{:S(2)}, u32[]{:S(2)}) collective-permute-start(bf16[1,64,2048]{2,1,0:T(8,128)(2,1)S(1)} %get-tuple-element.137), channel_id=1, source_target_pairs={{0,8},{4,12},{8,16},{12,20},{16,24},{20,28},{24,0},{28,4},{1,9},{5... | collective-permute-start | bytes 786440 | tf_op jit(solution)/shard_map/ppermute | solution.py:53
  390.4 14.2 %collective-permute-start.6 = (bf16[1,64,2048]{2,1,0:T(8,128)(2,1)S(1)}, bf16[1,64,2048]{2,1,0:T(8,128)(2,1)S(1)}, u32[]{:S(2)}, u32[]{:S(2)}) collective-permute-start(bf16[1,64,2048]{2,1,0:T(8,128)(2,1)S(1)} %get-tuple-element.136), channel_id=1, source_target_pairs={{0,4},{4,8},{8,12},{12,16},{16,20},{20,24},{24,28},{28,0},{1,5},{5... | collective-permute-start | bytes 786440 | tf_op jit(solution)/shard_map/ppermute | solution.py:53
Sparse Core Ops, SparseCore 0:
  10.3 163.3 all-gather.1
  223.1 144.3 reduce-scatter.1
